TPU v7x, 32 devices: a whole 2x2x4 slice. The times are simulated.
32 devices in a mesh: req: 8 (over z, y), tp: 4 (over x, core).
Axes of the slice: x: 2, y: 2, z: 4, core: 2. Of those that a mesh axis runs over, the one named last changes fastest.
Arguments:
- hidden: bfloat16 [4096, 2048], P('req', 'tp'), may hold values from -6 to 6
- queries: bfloat16 [4096, 2048], P('req', 'tp'), may hold values from -4 to 4
- new_keys: bfloat16 [4096, 512], P('req'), may hold values from -4 to 4
- new_values: bfloat16 [4096, 512], P('req'), may hold values from -6 to 6
- cache_keys: bfloat16 [384, 64, 512], P('req'), may hold values from -6 to 6
- cache_values: bfloat16 [384, 64, 512], P('req'), may hold values from -6 to 6
- out_weight: bfloat16 [2048, 2048], P('tp'), may hold values from -0.125 to 0.125
- attn_gain: bfloat16 [2048], P('tp'), may hold values from 0.099609375 to 1.8984375
- ple_input: bfloat16 [4096, 256], P('req'), may hold values from -6 to 6
- ple_gate_weight: bfloat16 [2048, 256], P('tp'), may hold values from -0.125 to 0.125
- ple_proj_weight: bfloat16 [256, 2048], P(None, 'tp'), may hold values from -0.375 to 0.375
- ple_gain: bfloat16 [2048], P('tp'), may hold values from 0.099609375 to 1.8984375
- page_holder: int32 [384, 1], P('req'), may hold values from 0 to 7; in each aligned block of 48 rows (0 to 47, 48 to 95, ...) at most 6 rows name the same one
- page_slot: int32 [384, 1], P('req'), may hold values from 0 to 47
- page_counts: int32 [8, 8], P('req'), may hold values from 1 to 12, 48 in all within a row
- last_fill: int32 [8, 8], P('req'), may hold values from 1 to 64
- row_counts: int32 [8, 8], P('req'), may hold values from 1 to 256, 512 in all within a row
Outputs:
- layer_out: bfloat16 [4096, 2048], P('req', 'tp')
Inputs may be any that keep to these rules, and one draw needn't show every extreme that they name: `page_holder`: within the 48 page references of one device's requests (aligned blocks), no req index is named more than 6 times; in some block one is named exactly 6 times. `page_counts`: the 8 counts of one device sum to 48; some count equals 12. `row_counts`: the 8 counts of one device sum to 512; some count equals 256.
All inputs are finite; a program needn't handle non-finite values.
Results may differ from a plain program's by a relative error of at most 0.0061.
Values may be sent and summed in bfloat16 or wider, within the bound.
No kernel may reach another device: no remote copies, remote signals or barrier semaphores. Data moves between devices by JAX's collectives and lax.ppermute only.
A program may use at most 128 MiB of HBM per device.

v0:
```python
import math
import jax
import jax.numpy as jnp
from jax import lax
from jax.sharding import PartitionSpec as P

D = 2048
HD = 256


def slot_lookup(positions, counts):
    starts = jnp.cumsum(counts) - counts
    owning = jnp.sum((positions[:, None] >= starts[None, :]).astype(jnp.int32), axis=1) - 1
    return (owning, starts)


def table_pick(table, owning):
    onehot = owning[:, None] == jnp.arange(table.shape[0], dtype=jnp.int32)[None, :]
    return jnp.sum(jnp.where(onehot, table[None, :], 0), axis=1)


def attend_masks(counts_of_pages, fill_row, counts_of_rows, page_len, page_total, row_total):
    key_index = jnp.arange(page_total * page_len, dtype=jnp.int32)
    page_ref = key_index // page_len
    within = key_index % page_len
    page_owner, page_starts = slot_lookup(page_ref, counts_of_pages)
    context_len = (counts_of_pages - 1) * page_len + fill_row
    position = (page_ref - table_pick(page_starts, page_owner)) * page_len + within
    valid = position < table_pick(context_len, page_owner)
    row_index = jnp.arange(row_total, dtype=jnp.int32)
    row_owner = slot_lookup(row_index, counts_of_rows)[0]
    context_mask = (row_owner[:, None] == page_owner[None, :]) & valid[None, :]
    causal = (row_owner[:, None] == row_owner[None, :]) & (row_index[None, :] <= row_index[:, None])
    return jnp.concatenate([context_mask, causal], axis=1)


def shards(
    hidden,
    queries,
    new_keys,
    new_values,
    cache_keys,
    cache_values,
    out_weight,
    attn_gain,
    ple_input,
    ple_gate_weight,
    ple_proj_weight,
    ple_gain,
    page_holder,
    page_slot,
    page_counts,
    last_fill,
    row_counts,
):
    row_total = hidden.shape[0]
    page_total = cache_keys.shape[0]
    page_len = cache_keys.shape[1]
    req_count = lax.axis_size("req")
    tp_index = lax.axis_index("tp")
    local_heads = queries.shape[1] // HD
    kv_head = tp_index // 2
    capacity = max(2, page_total // req_count)
    holders = page_holder[:, 0]
    places = page_slot[:, 0]
    ref_index = jnp.arange(page_total, dtype=jnp.int32)
    earlier = (holders[:, None] == holders[None, :]) & (ref_index[:, None] > ref_index[None, :])
    ranking = jnp.sum(earlier.astype(jnp.int32), axis=1)
    matched = (holders[:, None, None] == jnp.arange(req_count, dtype=jnp.int32)[None, :, None]) & (
        ranking[:, None, None] == jnp.arange(capacity, dtype=jnp.int32)[None, None, :]
    )
    request_table = jnp.sum(jnp.where(matched, places[:, None, None] + 1, 0), axis=0) - 1
    asked = lax.all_to_all(request_table, "req", split_axis=0, concat_axis=0, tiled=True)
    wanted = jnp.maximum(asked, 0)
    head_keys = lax.dynamic_slice_in_dim(cache_keys, kv_head * HD, HD, 2)
    head_values = lax.dynamic_slice_in_dim(cache_values, kv_head * HD, HD, 2)
    stacked = jnp.concatenate([head_keys, head_values], axis=2)
    arrival_index = holders * capacity + ranking
    outgoing = stacked[wanted]
    arrived = lax.all_to_all(outgoing, "req", split_axis=0, concat_axis=0, tiled=True)
    context = arrived.reshape(req_count * capacity, page_len, 2 * HD)[arrival_index]
    context_keys = context[:, :, :HD].reshape(page_total * page_len, HD)
    context_values = context[:, :, HD:].reshape(page_total * page_len, HD)
    fresh_keys = lax.dynamic_slice_in_dim(new_keys, kv_head * HD, HD, 1)
    fresh_values = lax.dynamic_slice_in_dim(new_values, kv_head * HD, HD, 1)
    all_keys = jnp.concatenate([context_keys, fresh_keys], axis=0)
    all_values = jnp.concatenate([context_values, fresh_values], axis=0)
    masking = attend_masks(
        page_counts[0], last_fill[0], row_counts[0], page_len, page_total, row_total
    )
    query_rows = queries.reshape(row_total, local_heads, HD)
    scores = jnp.einsum("rhd,kd->hrk", query_rows, all_keys, preferred_element_type=jnp.float32) * (
        1.0 / math.sqrt(HD)
    )
    scores = jnp.where(masking[None], scores, -1e30)
    highest = jnp.max(scores, axis=-1, keepdims=True)
    expo = jnp.exp(scores - highest)
    weights = (expo / jnp.sum(expo, axis=-1, keepdims=True)).astype(jnp.bfloat16)
    attention = jnp.einsum("hrk,kd->rhd", weights, all_values, preferred_element_type=jnp.float32)
    attention = attention.astype(jnp.bfloat16).reshape(row_total, local_heads * HD)
    tp_size = lax.axis_size("tp")
    full_weight = lax.all_gather(out_weight, "tp", axis=0, tiled=True)
    full_gate_weight = lax.all_gather(ple_gate_weight, "tp", axis=0, tiled=True)
    full_proj_weight = lax.all_gather(ple_proj_weight, "tp", axis=1, tiled=True)
    full_attn_gain = lax.all_gather(attn_gain, "tp", axis=0, tiled=True)
    full_ple_gain = lax.all_gather(ple_gain, "tp", axis=0, tiled=True)
    row_hidden = lax.all_to_all(hidden, "tp", split_axis=0, concat_axis=1, tiled=True)
    row_attention = lax.all_to_all(attention, "tp", split_axis=0, concat_axis=1, tiled=True)
    part_rows = row_attention.shape[0]
    row_ple = lax.dynamic_slice_in_dim(ple_input, tp_index * part_rows, part_rows, 0)
    projected = jnp.dot(row_attention, full_weight, preferred_element_type=jnp.float32)
    squares = jnp.sum(projected * projected, axis=1)
    normed = (
        projected
        * lax.rsqrt(squares / D + 1e-06)[:, None]
        * full_attn_gain.astype(jnp.float32)[None, :]
    )
    mixed_state = (row_hidden.astype(jnp.float32) + normed).astype(jnp.bfloat16)
    gate = jnp.dot(mixed_state, full_gate_weight, preferred_element_type=jnp.float32)
    activated = (jax.nn.gelu(gate, approximate=True) * row_ple.astype(jnp.float32)).astype(
        jnp.bfloat16
    )
    lifted = jnp.dot(activated, full_proj_weight, preferred_element_type=jnp.float32)
    lift_squares = jnp.sum(lifted * lifted, axis=1)
    lift_normed = (
        lifted
        * lax.rsqrt(lift_squares / D + 1e-06)[:, None]
        * full_ple_gain.astype(jnp.float32)[None, :]
    )
    row_out = (mixed_state.astype(jnp.float32) + lift_normed).astype(jnp.bfloat16)
    return lax.all_to_all(row_out, "tp", split_axis=1, concat_axis=0, tiled=True)


def solution(mesh):
    return jax.shard_map(
        shards,
        mesh=mesh,
        in_specs=(
            P("req", "tp"),
            P("req", "tp"),
            P("req", None),
            P("req", None),
            P("req", None, None),
            P("req", None, None),
            P("tp", None),
            P("tp"),
            P("req", None),
            P("tp", None),
            P(None, "tp"),
            P("tp"),
            P("req", None),
            P("req", None),
            P("req", None),
            P("req", None),
            P("req", None),
        ),
        out_specs=P("req", "tp"),
        check_vma=False,
    )
```

profile of v0, /device:TPU:0, one launch (start us, length us, event | category | flops | bytes accessed | tf_op | source)
XLA Modules:
  0.0 189.8 jit_solution(16006355638064620231)
XLA Ops:
  6.5 0.7 all-gather.6.cloned.1.call-update
  7.3 0.9 convert_reduce_fusion.1
  8.2 0.7 add_bitcast_fusion.2
  9.7 0.7 copy.41
  10.4 7.3 %all-to-all-start.1 = ((s32[8,1,6]{2,1,0:T(1,128)}), s32[8,1,6]{2,1,0:T(1,128)S(1)}, u32[]{:S(2)}, u32[]{:S(2)}) async-start(s32[8,1,6]{2,1,0:T(1,128)} %copy.41), calls=%async_computation.1 | async-start | bytes 8192 | tf_op jit(solution)/shard_map/all_to_all | solution.py:73
  17.7 2.7 %constant_dynamic-slice_fusion.2 = (bf16[48,64,256]{2,1,0:T(8,128)(2,1)S(1)}, bf16[48,64,256]{2,1,0:T(8,128)(2,1)S(1)}) fusion(bf16[48,64,512]{2,1,0:T(8,128)(2,1)} %param.22, s32[]{:T(128)S(6)} %select_n.60, bf16[48,64,512]{2,1,0:T(8,128)(2,1)} %param.21), kind=kLoop, calls=%fused_computation.83 | loop fusion | bytes 6291460 | tf_op jit(solution)/shard_map/dynamic_slice | solution.py:76
  20.6 3.4 %all-to-all-done.1 = s32[8,1,6]{2,1,0:T(1,128)S(1)} async-done(((s32[8,1,6]{2,1,0:T(1,128)}), s32[8,1,6]{2,1,0:T(1,128)S(1)}, u32[]{:S(2)}, u32[]{:S(2)}) %all-to-all-start.1) | async-done | bytes 224 | tf_op jit(solution)/shard_map/all_to_all | solution.py:73
  24.2 2.5 %gather_fusion = bf16[48,64,512]{2,1,0:T(8,128)(2,1)} fusion(bf16[48,64,512]{2,1,0:T(8,128)(2,1)S(1)} %pad_maximum_fusion, s32[1024]{0:T(1024)S(1)} %pad_clamp_fusion.1), kind=kCustom, calls=%fused_computation | custom fusion | bytes 6291648 | tf_op jit(solution)/shard_map/gather | solution.py:79
  26.7 3.8 %all-to-all-start.2 = ((bf16[8,6,64,512]{3,2,1,0:T(8,128)(2,1)}), bf16[8,6,64,512]{3,2,1,0:T(8,128)(2,1)S(1)}, u32[]{:S(2)}, u32[]{:S(2)}) async-start(bf16[8,6,64,512]{3,2,1,0:T(8,128)(2,1)} %bitcast.73), calls=%async_computation.2 | async-start | bytes 6291456 | tf_op jit(solution)/shard_map/all_to_all | solution.py:80
  30.5 0.7 all-gather.10.cloned.1.call-update
  31.6 1.8 constant_dynamic-slice_fusion
  33.4 0.8 copy.51
  34.8 2.4 %compare_and_fusion = pred[512,3072]{0,1:T(8,128)(4,1)S(1)} fusion(s32[512]{0:T(512)S(1)} %broadcast_add_fusion.1, s32[3072]{0:T(1024)S(1)} %broadcast_add_fusion, pred[3072]{0:T(1024)(128)(4,1)S(1)} %fusion.40), kind=kLoop, calls=%fused_computation.12 | loop fusion | flops 3145728 | bytes 1590272 | tf_op jit(solution)/shard_map/and | solution.py:32
  37.2 1.7 pad_add_fusion
  38.9 61.1 %all-to-all-done.2 = bf16[8,6,64,512]{3,2,1,0:T(8,128)(2,1)S(1)} async-done(((bf16[8,6,64,512]{3,2,1,0:T(8,128)(2,1)}), bf16[8,6,64,512]{3,2,1,0:T(8,128)(2,1)S(1)}, u32[]{:S(2)}, u32[]{:S(2)}) %all-to-all-start.2) | async-done | bytes 3145760 | tf_op jit(solution)/shard_map/all_to_all | solution.py:80
  100.0 4.1 %all-to-all-start = ((bf16[4,128,512]{2,1,0:T(8,128)(2,1)}), bf16[4,128,512]{2,1,0:T(8,128)(2,1)}, u32[]{:S(2)}, u32[]{:S(2)}) async-start(bf16[4,128,512]{2,1,0:T(8,128)(2,1)} %bitcast.82), calls=%async_computation | async-start | bytes 1048576 | tf_op jit(solution)/shard_map/all_to_all | solution.py:107
  104.1 2.5 %gather_fusion.1 = bf16[48,64,512]{2,1,0:T(8,128)(2,1)} fusion(bf16[48,64,512]{2,1,0:T(8,128)(2,1)S(1)} %bitcast.72, s32[1024]{0:T(1024)S(1)} %pad_clamp_fusion), kind=kCustom, calls=%fused_computation.1 | custom fusion | bytes 6291648 | tf_op jit(solution)/shard_map/gather | solution.py:81
  106.6 2.1 %fusion.52 = (bf16[48,64,256]{2,1,0:T(8,128)(2,1)S(1)}, bf16[48,64,256]{2,1,0:T(8,128)(2,1)S(1)}) fusion(bf16[48,64,512]{2,1,0:T(8,128)(2,1)} %gather_fusion.1), kind=kLoop, calls=%fused_computation.102 | loop fusion | bytes 6291456 | tf_op jit(solution)/shard_map/slice | solution.py:83
  108.7 1.8 copy.43
  110.5 8.6 %fusion.8 = f32[3584,512,2]{1,0,2:T(8,128)} fusion(bf16[512,256]{1,0:T(8,128)(2,1)} %get-tuple-element.17, bf16[3072,256]{1,0:T(8,128)(2,1)S(1)} %bitcast.74, bf16[64,2,8,256]{3,2,1,0:T(8,128)(2,1)} %bitcast.81), kind=kOutput, calls=%fused_computation.18 | convolution fusion | flops 1882718208 | bytes 17039360 | tf_op jit(solution)/shard_map/rhd,kd->hrk/dot_general | solution.py:92
  119.1 16.0 %fusion.53 = (f32[2,512]{1,0:T(2,128)S(1)}, f32[2,512,3584]{1,2,0:T(8,128)}) fusion(f32[3584,512,2]{1,0,2:T(8,128)} %fusion.8, pred[512,3584]{0,1:T(8,128)(4,1)S(1)} %copy-done), kind=kOutput, calls=%fused_computation.103 | output fusion | flops 22023680 | bytes 31199232 | tf_op jit(solution)/shard_map/sub | solution.py:97
  135.0 7.3 %fusion.12 = bf16[512,2,256]{0,2,1:T(8,128)(2,1)S(1)} fusion(f32[2,512,3584]{1,2,0:T(8,128)} %get-tuple-element.12, f32[2,512]{1,0:T(2,128)S(1)} %get-tuple-element.11, bf16[512,256]{0,1:T(8,128)(2,1)} %copy.51, bf16[3072,256]{0,1:T(8,128)(2,1)S(1)} %copy-done.1), kind=kOutput, calls=%fused_computation.22 | convolution fusion | flops 1890320384 | bytes 17043456 | tf_op jit(solution)/shard_map/hrk,kd->rhd/dot_general | solution.py:99
  142.5 0.9 copy.46
  143.4 3.7 %all-to-all-start.3 = ((bf16[4,128,512]{1,2,0:T(8,128)(2,1)}), bf16[4,128,512]{1,2,0:T(8,128)(2,1)S(1)}, u32[]{:S(2)}, u32[]{:S(2)}) async-start(bf16[4,128,512]{1,2,0:T(8,128)(2,1)} %copy.46), calls=%async_computation.3 | async-start | bytes 1048576 | tf_op jit(solution)/shard_map/all_to_all | solution.py:108
  147.1 0.7 all-gather.8.cloned.1.call-update
  147.8 9.0 %all-gather = bf16[4,1,512]{2,1,0:T(2,128)(2,1)S(1)} all-gather(bf16[1,1,512]{2,1,0:T(2,128)(2,1)S(1)} %reshape.210), channel_id=1, replica_groups=mesh['req'=8,'tp'=4] {'tp'}, dimensions={0}, use_global_device_ids=true | all-gather | bytes 5120 | tf_op jit(solution)/shard_map/all_gather | solution.py:105
  156.8 5.2 %all-gather.1 = bf16[4,1,512]{2,1,0:T(2,128)(2,1)S(1)} all-gather(bf16[1,1,512]{2,1,0:T(2,128)(2,1)S(1)} %reshape.212), channel_id=1, replica_groups=mesh['req'=8,'tp'=4] {'tp'}, dimensions={0}, use_global_device_ids=true | all-gather | bytes 5120 | tf_op jit(solution)/shard_map/all_gather | solution.py:106
  162.0 1.2 convert_bitcast_fusion
  163.4 4.8 %multiply_reduce_fusion.1 = (f32[128]{0:T(128)S(1)}, f32[128,2048]{1,0:T(8,128)S(1)}) fusion(bf16[128,2048]{0,1:T(8,128)(2,1)S(1)} %bitcast.77, bf16[2048,2048]{1,0:T(8,128)(2,1)} %all-gather.6.cloned.1.call-done), kind=kOutput, calls=%fused_computation.27 | convolution fusion | flops 1074265984 | bytes 9961984 | tf_op jit(solution)/shard_map/dot_general | solution.py:111
  168.4 2.5 %multiply_reduce_fusion = (f32[128]{0:T(128)S(1)}, f32[128,2048]{1,0:T(8,128)S(1)}) fusion(bf16[256,2048]{1,0:T(8,128)(2,1)} %all-gather.10.cloned.1.call-done, bf16[512,256]{1,0:T(8,128)(2,1)} %param.25, s32[]{:T(128)S(6)} %select_n.68, bf16[128,2048]{1,0:T(8,128)(2,1)S(1)} %add_convert_fusion.1, bf16[2048,256]{1,0:T(8,128)(2,1)} %all-gather.8.cloned.1.call-done), kind=kOutput, calls=%fused_computation.25 | convolution fusion | flops 269320064 | bytes 3736068 | tf_op jit(solution)/shard_map/dot_general | solution.py:123
  171.2 11.2 %all_to_all.62 = bf16[128,4,512]{2,0,1:T(8,128)(2,1)S(1)} all-to-all(bf16[128,4,512]{2,0,1:T(8,128)(2,1)S(1)} %bitcast.79), channel_id=1, replica_groups=mesh['req'=8,'tp'=4] {'tp'}, dimensions={1} | all-to-all | bytes 1048576 | tf_op jit(solution)/shard_map/all_to_all | solution.py:131
  182.4 0.8 copy.62
  (57 shorter events, 3.1 us)
Async XLA Ops:
  6.5 156.8 %all-gather.6.cloned.1.call-start = ((), (), s32[]{:S(2)}) async-start(), calls=%async_computation.5 | async-start | bytes 10485760 | tf_op jit(solution)/shard_map/all_gather | solution.py:102
  10.4 13.7 %all-to-all-start.1 = ((s32[8,1,6]{2,1,0:T(1,128)}), s32[8,1,6]{2,1,0:T(1,128)S(1)}, u32[]{:S(2)}, u32[]{:S(2)}) async-start(s32[8,1,6]{2,1,0:T(1,128)} %copy.41), calls=%async_computation.1 | async-start | bytes 8192 | tf_op jit(solution)/shard_map/all_to_all | solution.py:73
  26.7 4.6 %copy-start.5 = (s32[1,8]{1,0:T(1,128)S(1)}, s32[1,8]{1,0:T(1,128)}, u32[]{:S(2)}) copy-start(s32[1,8]{1,0:T(1,128)} %param.31) | copy-start | bytes 100
  26.7 4.8 %copy-start.7 = (s32[1,8]{1,0:T(1,128)S(1)}, s32[1,8]{1,0:T(1,128)}, u32[]{:S(2)}) copy-start(s32[1,8]{1,0:T(1,128)} %param.33) | copy-start | bytes 100
  26.7 7.5 %copy-start.6 = (s32[48,1]{0,1:T(1,128)S(1)}, s32[48,1]{0,1:T(1,128)}, u32[]{:S(2)}) copy-start(s32[48,1]{0,1:T(1,128)} %param.29) | copy-start | bytes 580
  26.7 7.7 %copy-start.4 = (s32[1,8]{1,0:T(1,128)S(1)}, s32[1,8]{1,0:T(1,128)}, u32[]{:S(2)}) copy-start(s32[1,8]{1,0:T(1,128)} %param.32) | copy-start | bytes 100
  26.7 73.3 %all-to-all-start.2 = ((bf16[8,6,64,512]{3,2,1,0:T(8,128)(2,1)}), bf16[8,6,64,512]{3,2,1,0:T(8,128)(2,1)S(1)}, u32[]{:S(2)}, u32[]{:S(2)}) async-start(bf16[8,6,64,512]{3,2,1,0:T(8,128)(2,1)} %bitcast.73), calls=%async_computation.2 | async-start | bytes 6291456 | tf_op jit(solution)/shard_map/all_to_all | solution.py:80
  30.5 137.9 %all-gather.10.cloned.1.call-start = ((), (), s32[]{:S(2)}) async-start(), calls=%async_computation.7 | async-start | bytes 1310720 | tf_op jit(solution)/shard_map/all_gather | solution.py:104
  100.0 43.4 %all-to-all-start = ((bf16[4,128,512]{2,1,0:T(8,128)(2,1)}), bf16[4,128,512]{2,1,0:T(8,128)(2,1)}, u32[]{:S(2)}, u32[]{:S(2)}) async-start(bf16[4,128,512]{2,1,0:T(8,128)(2,1)} %bitcast.82), calls=%async_computation | async-start | bytes 1048576 | tf_op jit(solution)/shard_map/all_to_all | solution.py:107
  110.5 8.6 %copy-start = (pred[512,3584]{0,1:T(8,128)(4,1)S(1)}, pred[512,3584]{0,1:T(8,128)(4,1)}, u32[]{:S(2)}) copy-start(pred[512,3584]{0,1:T(8,128)(4,1)} %pad_add_fusion) | copy-start | bytes 5505028
  119.1 16.0 %copy-start.1 = (bf16[3072,256]{0,1:T(8,128)(2,1)S(1)}, bf16[3072,256]{0,1:T(8,128)(2,1)}, u32[]{:S(2)}) copy-start(bf16[3072,256]{0,1:T(8,128)(2,1)} %copy.43) | copy-start | bytes 4718596
  142.4 5.4 %copy-start.2 = (bf16[512]{0:T(512)(128)(2,1)S(1)}, bf16[512]{0:T(512)(128)(2,1)}, u32[]{:S(2)}) copy-start(bf16[512]{0:T(512)(128)(2,1)} %param.24) | copy-start | bytes 3076
  142.4 14.4 %copy-start.3 = (bf16[512]{0:T(512)(128)(2,1)S(1)}, bf16[512]{0:T(512)(128)(2,1)}, u32[]{:S(2)}) copy-start(bf16[512]{0:T(512)(128)(2,1)} %param.28) | copy-start | bytes 3076
  143.4 19.9 %all-to-all-start.3 = ((bf16[4,128,512]{1,2,0:T(8,128)(2,1)}), bf16[4,128,512]{1,2,0:T(8,128)(2,1)S(1)}, u32[]{:S(2)}, u32[]{:S(2)}) async-start(bf16[4,128,512]{1,2,0:T(8,128)(2,1)} %copy.46), calls=%async_computation.3 | async-start | bytes 1048576 | tf_op jit(solution)/shard_map/all_to_all | solution.py:108
  147.1 21.4 %all-gather.8.cloned.1.call-start = ((), (), s32[]{:S(2)}) async-start(), calls=%async_computation.6 | async-start | bytes 1310720 | tf_op jit(solution)/shard_map/all_gather | solution.py:103
Sparse Core Ops, SparseCore 0:
  8.9 60.9 all-gather.5
  71.5 16.7 all-gather.9
  149.5 16.2 all-gather.7
where the time goes:
time: 190 us
  waiting for transfers between devices  66.7 us (35%)
  blocking collectives  25.4 us (13%)
  other arithmetic  25.3 us (13%)
  matrix products  23.1 us (12%)
  starting transfers between devices  19 us (10%)
  local copies, waits for them, and re-layouts  16.9 us (9%)
  between operations  13.4 us (7%)
    all_to_all x1, waiting for transfers between devices, shards(): lax.all_to_all(outgoing, 'req', split_axis=0, concat_axis=0, tiled=True)  61.1 us
    sub x1, other arithmetic, shards(): expo = jnp.exp(scores - highest)  16 us
    all_to_all x1, blocking collectives, shards(): lax.all_to_all(row_out, 'tp', split_axis=1, concat_axis=0, tiled=True)  11.2 us
    all_gather x1, blocking collectives, shards(): full_attn_gain = lax.all_gather(attn_gain, 'tp', axis=0, tiled=True)  8.99 us
    dot_general x1, matrix products, shards(): jnp.einsum('rhd,kd->hrk', query_rows, all_keys, preferred_element_type=jn...  8.55 us
    dot_general x1, matrix products, shards(): jnp.einsum('hrk,kd->rhd', weights, all_values, preferred_element_type=jnp...  7.33 us
    all_to_all x1, starting transfers between devices, shards(): lax.all_to_all(request_table, 'req', split_axis=0, concat_axis=0, tiled=T...  7.28 us
    all_gather x1, blocking collectives, shards(): full_ple_gain = lax.all_gather(ple_gain, 'tp', axis=0, tiled=True)  5.18 us
  transfers between devices with their start and end apart: 7, of which 2 were waited for; matrix products, arithmetic and copies ran while one was open for 32% of the time, Pallas kernels for 0%

commit v1 on v0

--- a/solution.py
+++ b/solution.py
@@ -104,7 +104,9 @@
     full_proj_weight = lax.all_gather(ple_proj_weight, "tp", axis=1, tiled=True)
     full_attn_gain = lax.all_gather(attn_gain, "tp", axis=0, tiled=True)
     full_ple_gain = lax.all_gather(ple_gain, "tp", axis=0, tiled=True)
-    row_hidden = lax.all_to_all(hidden, "tp", split_axis=0, concat_axis=1, tiled=True)
+    shards_2 = jnp.split(hidden, lax.axis_size("tp"), axis=0)
+    incoming = lax.all_to_all(jnp.stack(shards_2), "tp", 0, 0)
+    row_hidden = jnp.concatenate(incoming, axis=1)
     row_attention = lax.all_to_all(attention, "tp", split_axis=0, concat_axis=1, tiled=True)
     part_rows = row_attention.shape[0]
     row_ple = lax.dynamic_slice_in_dim(ple_input, tp_index * part_rows, part_rows, 0)

time: 190 us -> 190 us (level)
  waiting for transfers between devices: 66.7 us -> 64.7 us
    all_to_all x1, waiting for transfers between devices: 61.1 us -> 59.1 us  [shards(): lax.all_to_all(outgoing, 'req', split_axis=0, concat_axis=0, tiled=True)]
  transfers between devices with their start and end apart: 7 -> 7, of which waited for: 2 -> 2; matrix products, arithmetic and copies ran while one was open for 32% -> 34% of each run, Pallas kernels for 0% -> 0%
where the time goes in v1:
time: 190 us
  waiting for transfers between devices  64.7 us (34%)
  other arithmetic  26.2 us (14%)
  blocking collectives  25.4 us (13%)
  matrix products  23.2 us (12%)
  starting transfers between devices  18.9 us (10%)
  local copies, waits for them, and re-layouts  18 us (9%)
  between operations  13.4 us (7%)
    all_to_all x1, waiting for transfers between devices, shards(): lax.all_to_all(outgoing, 'req', split_axis=0, concat_axis=0, tiled=True)  59.1 us
    sub x1, other arithmetic, shards(): expo = jnp.exp(scores - highest)  16 us
    all_to_all x1, blocking collectives, shards(): lax.all_to_all(row_out, 'tp', split_axis=1, concat_axis=0, tiled=True)  11.2 us
    all_gather x1, blocking collectives, shards(): full_attn_gain = lax.all_gather(attn_gain, 'tp', axis=0, tiled=True)  8.99 us
    dot_general x1, matrix products, shards(): jnp.einsum('rhd,kd->hrk', query_rows, all_keys, preferred_element_type=jn...  8.58 us
    dot_general x1, matrix products, shards(): jnp.einsum('hrk,kd->rhd', weights, all_values, preferred_element_type=jnp...  7.33 us
    all_to_all x1, starting transfers between devices, shards(): lax.all_to_all(request_table, 'req', split_axis=0, concat_axis=0, tiled=T...  7.28 us
    all_gather x1, blocking collectives, shards(): full_ple_gain = lax.all_gather(ple_gain, 'tp', axis=0, tiled=True)  5.18 us
  transfers between devices with their start and end apart: 7, of which 2 were waited for; matrix products, arithmetic and copies ran while one was open for 34% of the time, Pallas kernels for 0%

profile of v1, /device:TPU:0, one launch (start us, length us, event | category | flops | bytes accessed | tf_op | source)
XLA Modules:
  0.0 189.8 jit_solution(9078734703025695744)
XLA Ops:
  6.5 0.7 all-gather.6.cloned.1.call-update
  7.3 0.9 convert_reduce_fusion.1
  10.4 7.3 %all-to-all-start.1 = ((s32[8,1,6]{2,1,0:T(1,128)}), s32[8,1,6]{2,1,0:T(1,128)S(1)}, u32[]{:S(2)}, u32[]{:S(2)}) async-start(s32[8,1,6]{2,1,0:T(1,128)} %copy.41), calls=%async_computation.1 | async-start | bytes 8192 | tf_op jit(solution)/shard_map/all_to_all | solution.py:73
  17.7 2.7 %constant_dynamic-slice_fusion.2 = (bf16[48,64,256]{2,1,0:T(8,128)(2,1)S(1)}, bf16[48,64,256]{2,1,0:T(8,128)(2,1)S(1)}) fusion(bf16[48,64,512]{2,1,0:T(8,128)(2,1)} %param.22, s32[]{:T(128)S(6)} %select_n.60, bf16[48,64,512]{2,1,0:T(8,128)(2,1)} %param.21), kind=kLoop, calls=%fused_computation.88 | loop fusion | bytes 6291460 | tf_op jit(solution)/shard_map/dynamic_slice | solution.py:76
  20.6 3.4 %all-to-all-done.1 = s32[8,1,6]{2,1,0:T(1,128)S(1)} async-done(((s32[8,1,6]{2,1,0:T(1,128)}), s32[8,1,6]{2,1,0:T(1,128)S(1)}, u32[]{:S(2)}, u32[]{:S(2)}) %all-to-all-start.1) | async-done | bytes 224 | tf_op jit(solution)/shard_map/all_to_all | solution.py:73
  24.2 2.5 %gather_fusion = bf16[48,64,512]{2,1,0:T(8,128)(2,1)} fusion(bf16[48,64,512]{2,1,0:T(8,128)(2,1)S(1)} %pad_maximum_fusion, s32[1024]{0:T(1024)S(1)} %pad_clamp_fusion.1), kind=kCustom, calls=%fused_computation | custom fusion | bytes 6291648 | tf_op jit(solution)/shard_map/gather | solution.py:79
  26.7 3.8 %all-to-all-start.2 = ((bf16[8,6,64,512]{3,2,1,0:T(8,128)(2,1)}), bf16[8,6,64,512]{3,2,1,0:T(8,128)(2,1)S(1)}, u32[]{:S(2)}, u32[]{:S(2)}) async-start(bf16[8,6,64,512]{3,2,1,0:T(8,128)(2,1)} %bitcast.80), calls=%async_computation.2 | async-start | bytes 6291456 | tf_op jit(solution)/shard_map/all_to_all | solution.py:80
  30.5 0.7 all-gather.10.cloned.1.call-update
  31.6 1.8 constant_dynamic-slice_fusion
  33.4 0.8 copy.51
  34.6 1.1 slice_bitcast_fusion.3
  35.7 0.9 pad_maximum_fusion.1
  36.8 2.4 %compare_and_fusion = pred[512,3072]{0,1:T(8,128)(4,1)S(1)} fusion(s32[512]{0:T(512)S(1)} %broadcast_add_fusion.1, s32[3072]{0:T(1024)S(1)} %broadcast_add_fusion, pred[3072]{0:T(1024)(128)(4,1)S(1)} %fusion.40), kind=kLoop, calls=%fused_computation.12 | loop fusion | flops 3145728 | bytes 1590272 | tf_op jit(solution)/shard_map/and | solution.py:32
  39.2 1.6 pad_add_fusion
  40.8 59.1 %all-to-all-done.2 = bf16[8,6,64,512]{3,2,1,0:T(8,128)(2,1)S(1)} async-done(((bf16[8,6,64,512]{3,2,1,0:T(8,128)(2,1)}), bf16[8,6,64,512]{3,2,1,0:T(8,128)(2,1)S(1)}, u32[]{:S(2)}, u32[]{:S(2)}) %all-to-all-start.2) | async-done | bytes 3145760 | tf_op jit(solution)/shard_map/all_to_all | solution.py:80
  100.0 4.3 %all-to-all-start = ((bf16[4,128,512]{2,1,0:T(8,128)(2,1)}), bf16[4,128,512]{2,1,0:T(8,128)(2,1)}, u32[]{:S(2)}, u32[]{:S(2)}) async-start(bf16[4,128,512]{2,1,0:T(8,128)(2,1)} %pad_maximum_fusion.1), calls=%async_computation | async-start | bytes 1048576 | tf_op jit(solution)/shard_map/all_to_all | solution.py:108
  104.3 2.5 %gather_fusion.1 = bf16[48,64,512]{2,1,0:T(8,128)(2,1)} fusion(bf16[48,64,512]{2,1,0:T(8,128)(2,1)S(1)} %bitcast.79, s32[1024]{0:T(1024)S(1)} %pad_clamp_fusion), kind=kCustom, calls=%fused_computation.1 | custom fusion | bytes 6291648 | tf_op jit(solution)/shard_map/gather | solution.py:81
  106.8 2.1 %fusion.52 = (bf16[48,64,256]{2,1,0:T(8,128)(2,1)S(1)}, bf16[48,64,256]{2,1,0:T(8,128)(2,1)S(1)}) fusion(bf16[48,64,512]{2,1,0:T(8,128)(2,1)} %gather_fusion.1), kind=kLoop, calls=%fused_computation.107 | loop fusion | bytes 6291456 | tf_op jit(solution)/shard_map/slice | solution.py:83
  108.9 1.8 copy.43
  110.7 8.6 %fusion.8 = f32[3584,512,2]{1,0,2:T(8,128)} fusion(bf16[512,256]{1,0:T(8,128)(2,1)} %get-tuple-element.21, bf16[3072,256]{1,0:T(8,128)(2,1)S(1)} %bitcast.81, bf16[64,2,8,256]{3,2,1,0:T(8,128)(2,1)} %bitcast.88), kind=kOutput, calls=%fused_computation.18 | convolution fusion | flops 1882718208 | bytes 17039360 | tf_op jit(solution)/shard_map/rhd,kd->hrk/dot_general | solution.py:92
  119.3 16.0 %fusion.53 = (f32[2,512]{1,0:T(2,128)S(1)}, f32[2,512,3584]{1,2,0:T(8,128)}) fusion(f32[3584,512,2]{1,0,2:T(8,128)} %fusion.8, pred[512,3584]{0,1:T(8,128)(4,1)S(1)} %copy-done), kind=kOutput, calls=%fused_computation.108 | output fusion | flops 22023680 | bytes 31199232 | tf_op jit(solution)/shard_map/sub | solution.py:97
  135.3 7.3 %fusion.12 = bf16[512,2,256]{0,2,1:T(8,128)(2,1)S(1)} fusion(f32[2,512,3584]{1,2,0:T(8,128)} %get-tuple-element.16, f32[2,512]{1,0:T(2,128)S(1)} %get-tuple-element.15, bf16[512,256]{0,1:T(8,128)(2,1)} %copy.51, bf16[3072,256]{0,1:T(8,128)(2,1)S(1)} %copy-done.1), kind=kOutput, calls=%fused_computation.22 | convolution fusion | flops 1890320384 | bytes 17043456 | tf_op jit(solution)/shard_map/hrk,kd->rhd/dot_general | solution.py:99
  142.8 0.9 copy.46
  143.6 3.5 %all-to-all-start.3 = ((bf16[4,128,512]{1,2,0:T(8,128)(2,1)}), bf16[4,128,512]{1,2,0:T(8,128)(2,1)S(1)}, u32[]{:S(2)}, u32[]{:S(2)}) async-start(bf16[4,128,512]{1,2,0:T(8,128)(2,1)} %copy.46), calls=%async_computation.3 | async-start | bytes 1048576 | tf_op jit(solution)/shard_map/all_to_all | solution.py:110
  147.2 0.7 all-gather.8.cloned.1.call-update
  147.9 9.0 %all-gather = bf16[4,1,512]{2,1,0:T(2,128)(2,1)S(1)} all-gather(bf16[1,1,512]{2,1,0:T(2,128)(2,1)S(1)} %reshape.209), channel_id=1, replica_groups=mesh['req'=8,'tp'=4] {'tp'}, dimensions={0}, use_global_device_ids=true | all-gather | bytes 5120 | tf_op jit(solution)/shard_map/all_gather | solution.py:105
  156.9 5.2 %all-gather.1 = bf16[4,1,512]{2,1,0:T(2,128)(2,1)S(1)} all-gather(bf16[1,1,512]{2,1,0:T(2,128)(2,1)S(1)} %reshape.211), channel_id=1, replica_groups=mesh['req'=8,'tp'=4] {'tp'}, dimensions={0}, use_global_device_ids=true | all-gather | bytes 5120 | tf_op jit(solution)/shard_map/all_gather | solution.py:106
  162.1 1.2 convert_bitcast_fusion
  163.4 4.8 %multiply_reduce_fusion.1 = (f32[128]{0:T(128)S(1)}, f32[128,2048]{1,0:T(8,128)S(1)}) fusion(bf16[128,2048]{0,1:T(8,128)(2,1)S(1)} %bitcast.84, bf16[2048,2048]{1,0:T(8,128)(2,1)} %all-gather.6.cloned.1.call-done), kind=kOutput, calls=%fused_computation.27 | convolution fusion | flops 1074265984 | bytes 9961984 | tf_op jit(solution)/shard_map/dot_general | solution.py:113
  168.5 2.5 %multiply_reduce_fusion = (f32[128]{0:T(128)S(1)}, f32[128,2048]{1,0:T(8,128)S(1)}) fusion(bf16[256,2048]{1,0:T(8,128)(2,1)} %all-gather.10.cloned.1.call-done, bf16[512,256]{1,0:T(8,128)(2,1)} %param.25, s32[]{:T(128)S(6)} %select_n.68, bf16[128,2048]{1,0:T(8,128)(2,1)S(1)} %add_convert_fusion.1, bf16[2048,256]{1,0:T(8,128)(2,1)} %all-gather.8.cloned.1.call-done), kind=kOutput, calls=%fused_computation.25 | convolution fusion | flops 269320064 | bytes 3736068 | tf_op jit(solution)/shard_map/dot_general | solution.py:125
  171.2 11.2 %all_to_all.54 = bf16[128,4,512]{2,0,1:T(8,128)(2,1)S(1)} all-to-all(bf16[128,4,512]{2,0,1:T(8,128)(2,1)S(1)} %bitcast.86), channel_id=1, replica_groups=mesh['req'=8,'tp'=4] {'tp'}, dimensions={1} | all-to-all | bytes 1048576 | tf_op jit(solution)/shard_map/all_to_all | solution.py:133
  182.5 0.8 copy.62
  (59 shorter events, 4.4 us)
Async XLA Ops:
  6.5 156.9 %all-gather.6.cloned.1.call-start = ((), (), s32[]{:S(2)}) async-start(), calls=%async_computation.5 | async-start | bytes 10485760 | tf_op jit(solution)/shard_map/all_gather | solution.py:102
  10.4 13.7 %all-to-all-start.1 = ((s32[8,1,6]{2,1,0:T(1,128)}), s32[8,1,6]{2,1,0:T(1,128)S(1)}, u32[]{:S(2)}, u32[]{:S(2)}) async-start(s32[8,1,6]{2,1,0:T(1,128)} %copy.41), calls=%async_computation.1 | async-start | bytes 8192 | tf_op jit(solution)/shard_map/all_to_all | solution.py:73
  26.7 4.6 %copy-start.5 = (s32[1,8]{1,0:T(1,128)S(1)}, s32[1,8]{1,0:T(1,128)}, u32[]{:S(2)}) copy-start(s32[1,8]{1,0:T(1,128)} %param.31) | copy-start | bytes 100
  26.7 4.8 %copy-start.7 = (s32[1,8]{1,0:T(1,128)S(1)}, s32[1,8]{1,0:T(1,128)}, u32[]{:S(2)}) copy-start(s32[1,8]{1,0:T(1,128)} %param.33) | copy-start | bytes 100
  26.7 7.5 %copy-start.6 = (s32[48,1]{0,1:T(1,128)S(1)}, s32[48,1]{0,1:T(1,128)}, u32[]{:S(2)}) copy-start(s32[48,1]{0,1:T(1,128)} %param.29) | copy-start | bytes 580
  26.7 7.7 %copy-start.4 = (s32[1,8]{1,0:T(1,128)S(1)}, s32[1,8]{1,0:T(1,128)}, u32[]{:S(2)}) copy-start(s32[1,8]{1,0:T(1,128)} %param.32) | copy-start | bytes 100
  26.7 73.3 %all-to-all-start.2 = ((bf16[8,6,64,512]{3,2,1,0:T(8,128)(2,1)}), bf16[8,6,64,512]{3,2,1,0:T(8,128)(2,1)S(1)}, u32[]{:S(2)}, u32[]{:S(2)}) async-start(bf16[8,6,64,512]{3,2,1,0:T(8,128)(2,1)} %bitcast.80), calls=%async_computation.2 | async-start | bytes 6291456 | tf_op jit(solution)/shard_map/all_to_all | solution.py:80
  30.5 138.0 %all-gather.10.cloned.1.call-start = ((), (), s32[]{:S(2)}) async-start(), calls=%async_computation.7 | async-start | bytes 1310720 | tf_op jit(solution)/shard_map/all_gather | solution.py:104
  100.0 43.7 %all-to-all-start = ((bf16[4,128,512]{2,1,0:T(8,128)(2,1)}), bf16[4,128,512]{2,1,0:T(8,128)(2,1)}, u32[]{:S(2)}, u32[]{:S(2)}) async-start(bf16[4,128,512]{2,1,0:T(8,128)(2,1)} %pad_maximum_fusion.1), calls=%async_computation | async-start | bytes 1048576 | tf_op jit(solution)/shard_map/all_to_all | solution.py:108
  110.7 8.6 %copy-start = (pred[512,3584]{0,1:T(8,128)(4,1)S(1)}, pred[512,3584]{0,1:T(8,128)(4,1)}, u32[]{:S(2)}) copy-start(pred[512,3584]{0,1:T(8,128)(4,1)} %pad_add_fusion) | copy-start | bytes 5505028
  119.3 16.0 %copy-start.1 = (bf16[3072,256]{0,1:T(8,128)(2,1)S(1)}, bf16[3072,256]{0,1:T(8,128)(2,1)}, u32[]{:S(2)}) copy-start(bf16[3072,256]{0,1:T(8,128)(2,1)} %copy.43) | copy-start | bytes 4718596
  142.6 5.2 %copy-start.2 = (bf16[512]{0:T(512)(128)(2,1)S(1)}, bf16[512]{0:T(512)(128)(2,1)}, u32[]{:S(2)}) copy-start(bf16[512]{0:T(512)(128)(2,1)} %param.24) | copy-start | bytes 3076
  142.6 14.3 %copy-start.3 = (bf16[512]{0:T(512)(128)(2,1)S(1)}, bf16[512]{0:T(512)(128)(2,1)}, u32[]{:S(2)}) copy-start(bf16[512]{0:T(512)(128)(2,1)} %param.28) | copy-start | bytes 3076
  143.6 19.7 %all-to-all-start.3 = ((bf16[4,128,512]{1,2,0:T(8,128)(2,1)}), bf16[4,128,512]{1,2,0:T(8,128)(2,1)S(1)}, u32[]{:S(2)}, u32[]{:S(2)}) async-start(bf16[4,128,512]{1,2,0:T(8,128)(2,1)} %copy.46), calls=%async_computation.3 | async-start | bytes 1048576 | tf_op jit(solution)/shard_map/all_to_all | solution.py:110
  147.1 21.4 %all-gather.8.cloned.1.call-start = ((), (), s32[]{:S(2)}) async-start(), calls=%async_computation.6 | async-start | bytes 1310720 | tf_op jit(solution)/shard_map/all_gather | solution.py:103
Sparse Core Ops, SparseCore 0:
  8.9 60.9 all-gather.5
  71.5 16.7 all-gather.9
  149.5 16.2 all-gather.7
